TPU v7x, 256 devices: a whole 4x4x8 slice. The times are simulated.
256 devices in a mesh: req: 32 (over x, z), tp: 8 (over y, core).
Axes of the slice: x: 4, y: 4, z: 8, core: 2. Of those that a mesh axis runs over, the one named last changes fastest.
Arguments:
- hidden: bfloat16 [4096, 2048], P('req', 'tp'), may hold values from -3 to 3
- lengths: int32 [4096], P('req'), may hold values from 1 to 1921, as said below
- routes: int32 [4096, 6], P('req'), may hold values from 0 to 63, all different within a row; in each aligned block of 128 rows (0 to 127, 128 to 255, ...) at most 32 rows name the same one
- latent_cache: bfloat16 [65536, 576], P('req'), may hold values from -400 to 400
- attention_gain: bfloat16 [2048], replicated, may hold values from 0.099609375 to 1.8984375
- query_weight: bfloat16 [2048, 3072], P(None, 'tp'), may hold values from -0.125 to 0.125
- latent_weight: bfloat16 [2048, 576], P(None, 'tp'), may hold values from -0.125 to 0.125
- latent_gain: bfloat16 [512], replicated, may hold values from 0.099609375 to 1.8984375
- key_absorb: bfloat16 [16, 128, 512], P('tp'), may hold values from -0.5 to 0.5
- value_absorb: bfloat16 [16, 512, 128], P('tp'), may hold values from -0.5 to 0.5
- output_weight: bfloat16 [2048, 2048], P('tp'), may hold values from -0.75 to 0.75
- feedforward_gain: bfloat16 [2048], replicated, may hold values from 0.099609375 to 1.8984375
- router_weight: bfloat16 [2048, 64], replicated, may hold values from -0.0625 to 0.0625
- expert_gate: bfloat16 [64, 2048, 1408], P('req', None, 'tp'), may hold values from -0.25 to 0.25
- expert_up: bfloat16 [64, 2048, 1408], P('req', None, 'tp'), may hold values from -0.25 to 0.25
- expert_down: bfloat16 [64, 1408, 2048], P('req', 'tp'), may hold values from -0.4375 to 0.4375
- shared_gate: bfloat16 [2048, 1408], P(None, 'tp'), may hold values from -0.25 to 0.25
- shared_up: bfloat16 [2048, 1408], P(None, 'tp'), may hold values from -0.25 to 0.25
- shared_down: bfloat16 [1408, 2048], P('tp'), may hold values from -0.21875 to 0.21875
Outputs:
- next_hidden: bfloat16 [4096, 2048], P('req', 'tp')
- new_rows: bfloat16 [4096, 576], P('req')
Inputs may be any that keep to these rules, and one draw needn't show every extreme that they name: The lengths of the 128 requests of one index of req (aligned blocks of 128) sum to at most 2048, and to exactly 2048 on some index, where one request holds 1921. `routes`: among the rows of one index of req, no expert is named by more than 32 rows, a bound that some block reaches.
All inputs are finite; a program needn't handle non-finite values.
Results may differ from a plain program's by a relative error of at most 0.023.
The roundings to bfloat16 on the way count: a program that leaves them out, or rounds other values in their place, can miss the bound.
Values may be sent and summed in bfloat16 or wider, within the bound.
No kernel may reach another device: no remote copies, remote signals or barrier semaphores. Data moves between devices by JAX's collectives and lax.ppermute only.
A program may use at most 128 MiB of HBM per device.

v0:
```python
import jax
import jax.numpy as jnp
from jax import lax
from jax.sharding import PartitionSpec as P

rope_base = 50000.0
route_scale = 2.446
norm_eps = 1e-06


def rms_norm(values, gains):
    widened = values.astype(jnp.float32)
    factor = lax.rsqrt(jnp.mean(widened * widened, axis=-1, keepdims=True) + norm_eps)
    return widened * factor * gains.astype(jnp.float32)


def rotate(values, positions):
    half_width = values.shape[-1] // 2
    exponent = jnp.arange(half_width, dtype=jnp.float32) * (2.0 / values.shape[-1])
    angles = positions[..., None] * jnp.power(rope_base, -exponent)
    cosine = jnp.cos(angles)
    sine_part = jnp.sin(angles)
    first_half = values[..., :half_width]
    second_half = values[..., half_width:]
    return jnp.concatenate(
        [
            first_half * cosine - second_half * sine_part,
            first_half * sine_part + second_half * cosine,
        ],
        axis=-1,
    )


def attend(queries, cache_rows, lengths, new_rows, score_scale, latent_width):
    starts = jnp.cumsum(lengths) - lengths
    places = jnp.arange(cache_rows.shape[0], dtype=jnp.int32)
    inside = (places[None, :] >= starts[:, None]) & (places[None, :] < (starts + lengths)[:, None])
    scores = (
        jnp.einsum("rhk,jk->rhj", queries, cache_rows, preferred_element_type=jnp.float32)
        * score_scale
    )
    own_score = (
        jnp.einsum("rhk,rk->rh", queries, new_rows, preferred_element_type=jnp.float32)
        * score_scale
    )
    highest = jnp.maximum(
        jnp.max(jnp.where(inside[:, None, :], scores, -jnp.inf), axis=-1), own_score
    )
    weights = jnp.where(inside[:, None, :], jnp.exp(scores - highest[..., None]), 0.0)
    own_weight = jnp.exp(own_score - highest)
    totals = jnp.sum(weights, axis=-1) + own_weight
    probabilities = (weights / totals[..., None]).astype(jnp.bfloat16)
    own_prob = (own_weight / totals).astype(jnp.bfloat16)
    summed = jnp.einsum(
        "rhj,jl->rhl",
        probabilities,
        cache_rows[:, :latent_width],
        preferred_element_type=jnp.float32,
    )
    summed = summed + own_prob.astype(jnp.float32)[..., None] * new_rows[
        :, None, :latent_width
    ].astype(jnp.float32)
    return summed.astype(jnp.bfloat16)


def shards(
    hidden,
    lengths,
    routes,
    latent_cache,
    attention_gain,
    query_weight,
    latent_weight,
    latent_gain,
    key_absorb,
    value_absorb,
    output_weight,
    feedforward_gain,
    router_weight,
    expert_gate,
    expert_up,
    expert_down,
    shared_gate,
    shared_up,
    shared_down,
):
    token_count = hidden.shape[0]
    owner_count = lax.axis_size("req")
    column_width = hidden.shape[1]
    column_start = lax.axis_index("tp") * column_width
    heads_here = key_absorb.shape[0]
    nope_width = key_absorb.shape[1]
    latent_width = key_absorb.shape[2]
    whole = lax.all_gather(hidden, "tp", axis=1, tiled=True)
    normed = rms_norm(whole, attention_gain).astype(jnp.bfloat16)
    projected = jnp.dot(normed, query_weight, preferred_element_type=jnp.float32).reshape(
        token_count, heads_here, -1
    )
    rope_width = projected.shape[2] - nope_width
    positions = lengths.astype(jnp.float32)
    query_nope = projected[..., :nope_width].astype(jnp.bfloat16)
    query_rope = rotate(projected[..., nope_width:], positions[:, None]).astype(jnp.bfloat16)
    query_latent = jnp.einsum(
        "thn,hnl->thl", query_nope, key_absorb, preferred_element_type=jnp.float32
    ).astype(jnp.bfloat16)
    latent_part = jnp.dot(normed, latent_weight, preferred_element_type=jnp.float32).astype(
        jnp.bfloat16
    )
    latent_raw = lax.all_gather(latent_part, "tp", axis=1, tiled=True)
    latent_new = rms_norm(latent_raw[:, :latent_width], latent_gain)
    key_new = rotate(latent_raw[:, latent_width:].astype(jnp.float32), positions)
    new_rows = jnp.concatenate([latent_new, key_new], axis=-1).astype(jnp.bfloat16)
    queries = jnp.concatenate([query_latent, query_rope], axis=-1)
    attended = attend(
        queries, latent_cache, lengths, new_rows, (nope_width + rope_width) ** (-0.5), latent_width
    )
    head_values = jnp.einsum(
        "thl,hlv->thv", attended, value_absorb, preferred_element_type=jnp.float32
    ).astype(jnp.bfloat16)
    attention = jnp.dot(
        head_values.reshape(token_count, -1), output_weight, preferred_element_type=jnp.float32
    )
    total_attention = lax.psum(attention, "tp")
    mixed = (whole.astype(jnp.float32) + total_attention).astype(jnp.bfloat16)
    mixed_columns = lax.dynamic_slice_in_dim(mixed, column_start, column_width, 1)
    expert_in = rms_norm(mixed, feedforward_gain).astype(jnp.bfloat16)
    logits = jnp.dot(expert_in, router_weight, preferred_element_type=jnp.float32)
    expert_count = router_weight.shape[1]
    top_count = routes.shape[1]
    per_owner = expert_count // owner_count
    slot_count = max(2, 8 * token_count * top_count // (3 * expert_count))
    chosen = jnp.take_along_axis(jax.nn.sigmoid(logits), routes, axis=1)
    route_weights = chosen / jnp.sum(chosen, axis=1, keepdims=True) * route_scale
    expert_ids = routes.reshape(-1)
    onehot = (expert_ids[:, None] == jnp.arange(expert_count, dtype=jnp.int32)[None, :]).astype(
        jnp.int32
    )
    earlier = jnp.cumsum(onehot, axis=0) - onehot
    slot_index = jnp.sum(earlier * onehot, axis=1)
    slot_places = (expert_ids * slot_count + slot_index).reshape(token_count, top_count)
    slot_total = expert_count * slot_count
    placed = slot_places[None, :, :] == jnp.arange(slot_total, dtype=jnp.int32)[:, None, None]
    gather_matrix = jnp.any(placed, axis=2).astype(jnp.bfloat16)
    combine_matrix = jnp.sum(jnp.where(placed, route_weights[None, :, :], 0.0), axis=2).T
    outgoing = jnp.dot(gather_matrix, expert_in, preferred_element_type=jnp.float32).astype(
        jnp.bfloat16
    )
    outgoing = outgoing.reshape(owner_count, per_owner, slot_count, expert_in.shape[1])
    slab = lax.all_to_all(outgoing, "req", split_axis=0, concat_axis=0, tiled=True)
    gate_part = jnp.einsum("oesd,edf->oesf", slab, expert_gate, preferred_element_type=jnp.float32)
    up_part = jnp.einsum("oesd,edf->oesf", slab, expert_up, preferred_element_type=jnp.float32)
    inner_units = (jax.nn.silu(gate_part) * up_part).astype(jnp.bfloat16)
    partial_out = jnp.einsum(
        "oesf,efd->oesd", inner_units, expert_down, preferred_element_type=jnp.float32
    )
    results = lax.psum_scatter(partial_out, "tp", scatter_dimension=3, tiled=True)
    shared_inner = (
        jax.nn.silu(jnp.dot(expert_in, shared_gate, preferred_element_type=jnp.float32))
        * jnp.dot(expert_in, shared_up, preferred_element_type=jnp.float32)
    ).astype(jnp.bfloat16)
    shared_part = jnp.dot(shared_inner, shared_down, preferred_element_type=jnp.float32)
    returned = lax.all_to_all(results, "req", split_axis=0, concat_axis=0, tiled=True)
    routed = jnp.dot(
        combine_matrix, returned.reshape(slot_total, column_width), precision=lax.Precision.HIGHEST
    )
    shared_columns = lax.psum_scatter(shared_part, "tp", scatter_dimension=1, tiled=True)
    next_hidden = (mixed_columns.astype(jnp.float32) + routed + shared_columns).astype(jnp.bfloat16)
    return (next_hidden, new_rows)


def solution(mesh):
    in_specs = (
        P("req", "tp"),
        P("req"),
        P("req", None),
        P("req", None),
        P(),
        P(None, "tp"),
        P(None, "tp"),
        P(),
        P("tp", None, None),
        P("tp", None, None),
        P("tp", None),
        P(),
        P(),
        P("req", None, "tp"),
        P("req", None, "tp"),
        P("req", "tp", None),
        P(None, "tp"),
        P(None, "tp"),
        P("tp", None),
    )
    out_specs = (P("req", "tp"), P("req", None))
    return jax.shard_map(shards, mesh=mesh, in_specs=in_specs, out_specs=out_specs, check_vma=False)
```

profile of v0, /device:TPU:1, one launch (start us, length us, event | category | flops | bytes accessed | tf_op | source)
XLA Modules:
  0.0 509.0 jit_solution(7842593407011253523)
XLA Ops:
  7.2 0.0 all-reduce.2.cloned.1.call-start
  7.2 16.5 %all_gather.6 = bf16[128,2048]{1,0:T(8,128)(2,1)S(1)} all-gather(bf16[128,256]{1,0:T(8,128)(2,1)} %param.19), channel_id=1, replica_groups=mesh['req'=32,'tp'=8] {'tp'}, dimensions={1}, use_global_device_ids=true | all-gather | bytes 589824 | tf_op jit(solution)/shard_map/all_gather | solution.py:94
  23.7 0.2 fusion.45
  23.9 0.7 convert_element_type.92
  24.6 1.3 convolution_convert_fusion.2
  26.0 12.8 %all_gather.7 = bf16[128,576]{0,1:T(8,128)(2,1)S(1)} all-gather(bf16[128,72]{0,1:T(8,128)(2,1)S(1)} %convolution_convert_fusion.2), channel_id=1, replica_groups=mesh['req'=32,'tp'=8] {'tp'}, dimensions={1}, use_global_device_ids=true | all-gather | bytes 165888 | tf_op jit(solution)/shard_map/all_gather | solution.py:109
  38.7 0.1 fusion.60
  38.9 0.1 copy.105
  39.0 0.2 reduce-window.18
  39.2 0.1 reduce.1
  39.3 0.5 copy-done.8
  39.8 0.5 fusion.94
  40.3 0.1 fusion.62
  40.5 0.8 copy.114
  41.3 0.1 subtract_convert_fusion.1
  41.5 0.1 copy.140
  41.7 0.7 copy.109
  42.4 0.7 copy.111
  43.1 0.8 fusion.70
  43.9 0.1 copy.137
  44.0 0.1 copy.138
  44.1 0.3 fusion.31
  44.4 1.1 fusion.56
  45.5 0.9 subtract_convert_fusion
  46.4 0.2 multiply_reduce_fusion
  46.6 2.9 select_reduce_fusion.1
  49.5 1.3 copy-done.2
  50.9 0.6 fusion.13
  51.4 3.5 fusion.34
  55.0 1.4 fusion.95
  56.4 0.0 reduce-scatter.3.cloned.1.call-start
  56.4 0.1 copy.116
  56.5 0.1 eq.42
  56.7 0.1 eq.38
  56.9 1.8 reduce-window.19
  58.7 0.3 slice_reduce_fusion
  59.0 0.1 fusion.67
  59.1 0.1 reduce_sum.69
  59.2 0.1 copy.119
  59.3 1.1 fusion.4
  60.4 62.6 %all-reduce.2.cloned.1.call-done = f32[128,2048]{1,0:T(8,128)} async-done(((f32[128,2048]{1,0:T(8,128)}), f32[128,2048]{1,0:T(8,128)}) %all-reduce.2.cloned.1.call-update) | async-done | bytes 1048592 | tf_op jit(solution)/shard_map/psum | solution.py:123
  123.0 1.5 fusion.42
  124.4 2.4 convolution_convert_fusion
  126.9 190.3 %all_to_all.10 = bf16[32,2,32,2048]{3,2,1,0:T(8,128)(2,1)S(1)} all-to-all(bf16[32,2,32,2048]{3,2,1,0:T(8,128)(2,1)S(1)} %bitcast.104), channel_id=1, replica_groups=mesh['req'=32,'tp'=8] {'req'}, dimensions={0} | all-to-all | bytes 16777216 | tf_op jit(solution)/shard_map/all_to_all | solution.py:149
  317.2 3.2 copy-done.1
  320.4 3.7 fusion.2
  324.1 15.2 %convolution_bitcast_fusion = f32[32,2,32,2048]{3,2,0,1:T(8,128)} fusion(f32[2,32,32,176]{3,2,1,0:T(8,128)} %fusion.2, bf16[32,2,32,2048]{3,2,1,0:T(8,128)(2,1)} %copy-done.1, bf16[2,176,2048]{2,1,0:T(8,128)(2,1)} %param.34, bf16[2,2048,176]{1,2,0:T(8,128)(2,1)} %param.33), kind=kOutput, calls=%fused_computation.6 | convolution fusion | flops 2954952704 | bytes 29491200 | tf_op jit(solution)/shard_map/oesf,efd->oesd/dot_general | solution.py:153
  339.3 0.0 reduce-scatter.3.cloned.1.call-update
  339.4 96.5 %reduce-scatter.3.cloned.1.call-done = f32[32,2,32,256]{3,2,0,1:T(8,128)} async-done(((f32[32,2,32,2048]{3,2,0,1:T(8,128)}), f32[32,2,32,256]{3,2,0,1:T(8,128)}) %reduce-scatter.3.cloned.1.call-update) | async-done | bytes 2097168 | tf_op jit(solution)/shard_map/reduce_scatter | solution.py:156
  435.8 3.2 copy.124
  439.0 9.8 %all-to-all-start.1 = ((f32[32,2,32,256]{3,2,1,0:T(8,128)}), f32[32,2,32,256]{3,2,1,0:T(8,128)}, u32[]{:S(2)}, u32[]{:S(2)}) async-start(f32[32,2,32,256]{3,2,1,0:T(8,128)} %copy.124), calls=%async_computation.2 | async-start | bytes 4194304 | tf_op jit(solution)/shard_map/all_to_all | solution.py:162
  448.9 0.0 reduce-scatter.5.cloned.1.call-start
  448.9 1.5 fusion.88
  450.5 3.2 fusion.38
  453.7 0.1 copy.120
  453.8 0.1 reshape.227
  453.9 0.4 fusion.41
  454.3 5.1 %gather_fusion = f32[768]{0:T(1024)S(1)} fusion(f32[128,64]{0,1:T(8,128)S(1)} %fusion.41, s32[768]{0:T(1024)S(1)} %reshape.227), kind=kCustom, calls=%fused_computation | custom fusion | bytes 12288 | tf_op jit(solution)/shard_map/jit(take_along_axis)/gather | solution.py:132
  459.4 0.1 reshape.230
  459.6 0.1 copy.121
  459.7 1.8 select_reduce_fusion
  461.5 25.5 %reduce-scatter.5.cloned.1.call-done = f32[128,256]{1,0:T(8,128)} async-done(((f32[128,2048]{1,0:T(8,128)}), f32[128,256]{1,0:T(8,128)}) %reduce-scatter.5.cloned.1.call-update) | async-done | bytes 131088 | tf_op jit(solution)/shard_map/reduce_scatter | solution.py:166
  487.0 11.1 %all-to-all-done.1 = f32[32,2,32,256]{3,2,1,0:T(8,128)} async-done(((f32[32,2,32,256]{3,2,1,0:T(8,128)}), f32[32,2,32,256]{3,2,1,0:T(8,128)}, u32[]{:S(2)}, u32[]{:S(2)}) %all-to-all-start.1) | async-done | bytes 2097184 | tf_op jit(solution)/shard_map/all_to_all | solution.py:162
  498.1 4.3 fusion.33
  (44 shorter events, 0.3 us)
Async XLA Ops:
  7.2 35.9 %copy-start = (bf16[2048,384]{1,0:T(8,128)(2,1)S(1)}, bf16[2048,384]{1,0:T(8,128)(2,1)}, u32[]{:S(2)}) copy-start(bf16[2048,384]{1,0:T(8,128)(2,1)} %param.24) | copy-start | bytes 4718596
  7.2 31.7 %copy-start.11 = (bf16[512]{0:T(512)(128)(2,1)S(1)}, bf16[512]{0:T(512)(128)(2,1)}, u32[]{:S(2)}) copy-start(bf16[512]{0:T(512)(128)(2,1)} %param.26) | copy-start | bytes 3076
  7.2 31.7 %copy-start.10 = (s32[128]{0:T(128)S(1)}, s32[128]{0:T(128)}, u32[]{:S(2)}) copy-start(s32[128]{0:T(128)} %param.20) | copy-start | bytes 1540
  7.2 115.8 %all-reduce.2.cloned.1.call-start = ((), (), s32[]{:S(2)}) async-start(), calls=%async_computation.4 | async-start | bytes 2097152 | tf_op jit(solution)/shard_map/psum | solution.py:123
  39.3 0.6 copy-start.8
  40.5 3.6 copy-start.6
  41.5 4.0 copy-start.5
  49.5 1.4 copy-start.2
  51.4 3.5 copy-start.3
  54.9 1.5 copy-start.7
  55.0 4.3 copy-start.9
  56.4 379.5 %reduce-scatter.3.cloned.1.call-start = ((), (), s32[]{:S(2)}) async-start(), calls=%async_computation.5 | async-start | bytes 18874368 | tf_op jit(solution)/shard_map/reduce_scatter | solution.py:156
  126.9 193.5 %copy-start.12 = (bf16[2,2048,176]{1,2,0:T(8,128)(2,1)S(1)}, bf16[2,2048,176]{1,2,0:T(8,128)(2,1)}, u32[]{:S(2)}) copy-start(bf16[2,2048,176]{1,2,0:T(8,128)(2,1)} %param.32) | copy-start | bytes 4325380
  317.2 3.2 copy-start.1
  439.0 11.4 %copy-start.4 = (bf16[176,2048]{1,0:T(8,128)(2,1)S(1)}, bf16[176,2048]{1,0:T(8,128)(2,1)}, u32[]{:S(2)}) copy-start(bf16[176,2048]{1,0:T(8,128)(2,1)} %param.37) | copy-start | bytes 2162692
  439.0 59.1 %all-to-all-start.1 = ((f32[32,2,32,256]{3,2,1,0:T(8,128)}), f32[32,2,32,256]{3,2,1,0:T(8,128)}, u32[]{:S(2)}, u32[]{:S(2)}) async-start(f32[32,2,32,256]{3,2,1,0:T(8,128)} %copy.124), calls=%async_computation.2 | async-start | bytes 4194304 | tf_op jit(solution)/shard_map/all_to_all | solution.py:162
  448.9 38.1 %reduce-scatter.5.cloned.1.call-start = ((), (), s32[]{:S(2)}) async-start(), calls=%async_computation.6 | async-start | bytes 1179648 | tf_op jit(solution)/shard_map/reduce_scatter | solution.py:166
  450.5 3.5 copy-start.13
Sparse Core Ops, SparseCore 0:
  56.5 66.4 all-reduce.1
  339.5 96.3 reduce-scatter.2
  453.8 33.1 reduce-scatter.4
where the time goes:
time: 510 us; the launch traced here: 509 us
  blocking collectives  220 us (43%)
  waiting for transfers between devices  196 us (38%)
  matrix products  40.9 us (8%)
  local copies, waits for them, and re-layouts  17.5 us (3%)
  between operations  14.1 us (3%)
  other arithmetic  11.2 us (2%)
  starting transfers between devices  9.94 us (2%)
    all_to_all x1, blocking collectives, shards(): lax.all_to_all(outgoing, 'req', split_axis=0, concat_axis=0, tiled=True)  190 us
    reduce_scatter x1, waiting for transfers between devices, shards(): lax.psum_scatter(partial_out, 'tp', scatter_dimension=3, tiled=True)  96.5 us
    psum x1, waiting for transfers between devices, shards(): total_attention = lax.psum(attention, 'tp')  62.6 us
    reduce_scatter x1, waiting for transfers between devices, shards(): lax.psum_scatter(shared_part, 'tp', scatter_dimension=1, tiled=True)  25.5 us
    all_gather x1, blocking collectives, shards(): whole = lax.all_gather(hidden, 'tp', axis=1, tiled=True)  16.5 us
    dot_general x1, matrix products, shards(): jnp.einsum('oesf,efd->oesd', inner_units, expert_down, preferred_element_...  15.2 us
    all_gather x1, blocking collectives, shards(): latent_raw = lax.all_gather(latent_part, 'tp', axis=1, tiled=True)  12.8 us
    all_to_all x1, waiting for transfers between devices, shards(): lax.all_to_all(results, 'req', split_axis=0, concat_axis=0, tiled=True)  11.1 us
  transfers between devices with their start and end apart: 4, of which 4 were waited for; matrix products, arithmetic and copies ran while one was open for 3% of the time, Pallas kernels for 0%

commit v1 on v0

--- a/solution.py
+++ b/solution.py
@@ -6,6 +6,14 @@
 rope_base = 50000.0
 route_scale = 2.446
 norm_eps = 1e-06
+
+
+def sum_by_hops(value, axis):
+    size, total = (lax.axis_size(axis), value)
+    for reach in [1 << k for k in range(size.bit_length() - 1)]:
+        route = [(i, i ^ reach) for i in range(size)]
+        total = total + lax.ppermute(total, axis, route)
+    return total
 
 
 def rms_norm(values, gains):
@@ -120,7 +128,7 @@
     attention = jnp.dot(
         head_values.reshape(token_count, -1), output_weight, preferred_element_type=jnp.float32
     )
-    total_attention = lax.psum(attention, "tp")
+    total_attention = sum_by_hops(attention, "tp")
     mixed = (whole.astype(jnp.float32) + total_attention).astype(jnp.bfloat16)
     mixed_columns = lax.dynamic_slice_in_dim(mixed, column_start, column_width, 1)
     expert_in = rms_norm(mixed, feedforward_gain).astype(jnp.bfloat16)

time: 510 us -> 496 us (0.973)
  waiting for transfers between devices: 196 us -> 181 us
    psum x1 -> x0, waiting for transfers between devices: 62.6 us -> none  [shards(): total_attention = lax.psum(attention, 'tp')]
    ppermute x0 -> x3, waiting for transfers between devices: none -> 47.1 us  [sum_by_hops(): total = total + lax.ppermute(total, axis, route)]
    all_to_all x1, waiting for transfers between devices: 11.1 us -> 38.8 us  [shards(): lax.all_to_all(results, 'req', split_axis=0, concat_axis=0, tiled=True)]
    reduce_scatter x1, waiting for transfers between devices: 25.5 us -> 0.02 us  [shards(): lax.psum_scatter(shared_part, 'tp', scatter_dimension=1, tiled=True)]
  transfers between devices with their start and end apart: 4 -> 6, of which waited for: 4 -> 5; matrix products, arithmetic and copies ran while one was open for 3% -> 4% of each run, Pallas kernels for 0% -> 0%
where the time goes in v1:
time: 496 us; the launch traced here: 495 us
  blocking collectives  221 us (45%)
  waiting for transfers between devices  181 us (36%)
  matrix products  37.1 us (7%)
  local copies, waits for them, and re-layouts  16.8 us (3%)
  between operations  14.5 us (3%)
  other arithmetic  13.4 us (3%)
  starting transfers between devices  11.7 us (2%)
    all_to_all x1, blocking collectives, shards(): lax.all_to_all(outgoing, 'req', split_axis=0, concat_axis=0, tiled=True)  191 us
    reduce_scatter x1, waiting for transfers between devices, shards(): lax.psum_scatter(partial_out, 'tp', scatter_dimension=3, tiled=True)  94.8 us
    ppermute x3, waiting for transfers between devices, sum_by_hops(): total = total + lax.ppermute(total, axis, route)  47.1 us
    all_to_all x1, waiting for transfers between devices, shards(): lax.all_to_all(results, 'req', split_axis=0, concat_axis=0, tiled=True)  38.8 us
    all_gather x1, blocking collectives, shards(): whole = lax.all_gather(hidden, 'tp', axis=1, tiled=True)  16.5 us
    dot_general x1, matrix products, shards(): jnp.einsum('oesf,efd->oesd', inner_units, expert_down, preferred_element_...  15.2 us
    all_gather x1, blocking collectives, shards(): latent_raw = lax.all_gather(latent_part, 'tp', axis=1, tiled=True)  12.8 us
  transfers between devices with their start and end apart: 6, of which 5 were waited for; matrix products, arithmetic and copies ran while one was open for 4% of the time, Pallas kernels for 0%

profile of v1, /device:TPU:1, one launch (start us, length us, event | category | flops | bytes accessed | tf_op | source)
XLA Modules:
  0.0 495.1 jit_solution(10745163291549391996)
XLA Ops:
  7.2 16.5 %all_gather.6 = bf16[128,2048]{1,0:T(8,128)(2,1)S(1)} all-gather(bf16[128,256]{1,0:T(8,128)(2,1)} %param.19), channel_id=1, replica_groups=mesh['req'=32,'tp'=8] {'tp'}, dimensions={1}, use_global_device_ids=true | all-gather | bytes 589824 | tf_op jit(solution)/shard_map/all_gather | solution.py:102
  23.7 0.2 fusion.43
  23.9 0.7 convert_element_type.92
  24.6 1.3 convolution_convert_fusion.2
  26.0 12.8 %all_gather.7 = bf16[128,576]{0,1:T(8,128)(2,1)S(1)} all-gather(bf16[128,72]{0,1:T(8,128)(2,1)S(1)} %convolution_convert_fusion.2), channel_id=1, replica_groups=mesh['req'=32,'tp'=8] {'tp'}, dimensions={1}, use_global_device_ids=true | all-gather | bytes 165888 | tf_op jit(solution)/shard_map/all_gather | solution.py:117
  38.9 0.1 copy.105
  39.0 0.2 reduce-window.18
  39.2 0.1 reduce.1
  39.3 0.5 copy-done.11
  39.8 0.5 fusion.92
  40.3 0.1 fusion.60
  40.5 0.1 copy.114
  40.6 0.1 subtract_convert_fusion.1
  40.8 0.1 copy.140
  40.9 0.7 copy.109
  41.7 0.7 copy.111
  42.4 0.8 fusion.68
  43.2 0.1 copy.137
  43.3 0.1 copy.138
  43.4 0.3 fusion.31
  43.7 1.1 fusion.54
  44.8 0.9 subtract_convert_fusion
  45.7 0.2 multiply_reduce_fusion
  45.9 2.9 select_reduce_fusion.1
  48.8 1.3 copy-done.4
  50.1 0.6 fusion.13
  50.7 3.4 fusion.32
  54.2 0.3 fusion.93
  54.5 0.3 collective-permute-start
  54.8 2.5 collective-permute-done
  57.3 0.1 add.92
  57.4 0.1 collective-permute-start.1
  57.5 24.5 %collective-permute-done.1 = f32[128,2048]{1,0:T(8,128)S(1)} collective-permute-done((f32[128,2048]{1,0:T(8,128)S(1)}, f32[128,2048]{1,0:T(8,128)S(1)}, u32[]{:S(2)}, u32[]{:S(2)}) %collective-permute-start.1) | collective-permute-done | bytes 1048608 | tf_op jit(solution)/shard_map/ppermute | solution.py:15
  82.0 0.1 add.93
  82.2 1.5 collective-permute-start.2
  83.6 0.1 copy.116
  83.7 0.1 eq.42
  83.9 0.1 eq.38
  84.0 1.8 reduce-window.19
  85.8 0.3 slice_reduce_fusion
  86.1 0.1 fusion.65
  86.3 0.1 reduce_sum.69
  86.5 1.1 fusion.4
  87.6 20.1 %collective-permute-done.2 = f32[128,2048]{1,0:T(8,128)} collective-permute-done((f32[128,2048]{1,0:T(8,128)S(1)}, f32[128,2048]{1,0:T(8,128)}, u32[]{:S(2)}, u32[]{:S(2)}) %collective-permute-start.2) | collective-permute-done | bytes 1048608 | tf_op jit(solution)/shard_map/ppermute | solution.py:15
  107.7 1.8 fusion.40
  109.6 2.4 convolution_convert_fusion
  112.0 191.5 %all_to_all.10 = bf16[32,2,32,2048]{3,2,1,0:T(8,128)(2,1)S(1)} all-to-all(bf16[32,2,32,2048]{3,2,1,0:T(8,128)(2,1)S(1)} %bitcast.104), channel_id=1, replica_groups=mesh['req'=32,'tp'=8] {'req'}, dimensions={0} | all-to-all | bytes 16777216 | tf_op jit(solution)/shard_map/all_to_all | solution.py:157
  303.5 3.2 copy-done.2
  306.7 3.8 fusion.2
  310.6 15.2 %convolution_bitcast_fusion = f32[32,2,32,2048]{3,2,0,1:T(8,128)} fusion(f32[2,32,32,176]{3,2,1,0:T(8,128)} %fusion.2, bf16[32,2,32,2048]{3,2,1,0:T(8,128)(2,1)} %copy-done.2, bf16[2,176,2048]{2,1,0:T(8,128)(2,1)} %param.34, bf16[2,2048,176]{1,2,0:T(8,128)(2,1)} %param.33), kind=kOutput, calls=%fused_computation.6 | convolution fusion | flops 2954952704 | bytes 29491200 | tf_op jit(solution)/shard_map/oesf,efd->oesd/dot_general | solution.py:161
  325.8 94.8 %reduce-scatter.3.cloned.1.call-done = f32[32,2,32,256]{3,2,0,1:T(8,128)} async-done(((f32[32,2,32,2048]{3,2,0,1:T(8,128)}), f32[32,2,32,256]{3,2,0,1:T(8,128)}) %reduce-scatter.3.cloned.1.call-update) | async-done | bytes 2097168 | tf_op jit(solution)/shard_map/reduce_scatter | solution.py:164
  420.6 3.2 copy.124
  423.8 9.8 %all-to-all-start.1 = ((f32[32,2,32,256]{3,2,1,0:T(8,128)}), f32[32,2,32,256]{3,2,1,0:T(8,128)}, u32[]{:S(2)}, u32[]{:S(2)}) async-start(f32[32,2,32,256]{3,2,1,0:T(8,128)} %copy.124), calls=%async_computation.2 | async-start | bytes 4194304 | tf_op jit(solution)/shard_map/all_to_all | solution.py:170
  433.6 0.5 fusion.86
  434.1 2.0 fusion.36
  436.1 0.1 copy.120
  436.3 0.1 reshape.227
  436.4 0.4 fusion.39
  436.8 5.1 %gather_fusion = f32[768]{0:T(1024)S(1)} fusion(f32[128,64]{0,1:T(8,128)S(1)} %fusion.39, s32[768]{0:T(1024)S(1)} %reshape.227), kind=kCustom, calls=%fused_computation | custom fusion | bytes 12288 | tf_op jit(solution)/shard_map/jit(take_along_axis)/gather | solution.py:140
  441.9 0.1 reshape.230
  442.2 1.8 select_reduce_fusion
  444.0 38.8 %all-to-all-done.1 = f32[32,2,32,256]{3,2,1,0:T(8,128)} async-done(((f32[32,2,32,256]{3,2,1,0:T(8,128)}), f32[32,2,32,256]{3,2,1,0:T(8,128)}, u32[]{:S(2)}, u32[]{:S(2)}) %all-to-all-start.1) | async-done | bytes 2097184 | tf_op jit(solution)/shard_map/all_to_all | solution.py:170
  482.8 3.8 fusion.94
  486.6 1.6 add_convert_fusion
  (60 shorter events, 0.6 us)
Async XLA Ops:
  7.2 35.2 %copy-start = (bf16[2048,384]{1,0:T(8,128)(2,1)S(1)}, bf16[2048,384]{1,0:T(8,128)(2,1)}, u32[]{:S(2)}) copy-start(bf16[2048,384]{1,0:T(8,128)(2,1)} %param.24) | copy-start | bytes 4718596
  7.2 31.7 %copy-start.14 = (bf16[512]{0:T(512)(128)(2,1)S(1)}, bf16[512]{0:T(512)(128)(2,1)}, u32[]{:S(2)}) copy-start(bf16[512]{0:T(512)(128)(2,1)} %param.26) | copy-start | bytes 3076
  7.2 31.7 %copy-start.13 = (s32[128]{0:T(128)S(1)}, s32[128]{0:T(128)}, u32[]{:S(2)}) copy-start(s32[128]{0:T(128)} %param.20) | copy-start | bytes 1540
  7.2 413.4 %reduce-scatter.3.cloned.1.call-start = ((), (), s32[]{:S(2)}) async-start(), calls=%async_computation.4 | async-start | bytes 18874368 | tf_op jit(solution)/shard_map/reduce_scatter | solution.py:164
  39.3 0.6 copy-start.11
  40.5 2.9 copy-start.9
  40.8 4.0 copy-start.8
  48.8 1.4 copy-start.4
  48.8 1.9 copy-start.17
  50.7 3.5 copy-start.5
  54.5 2.7 collective-permute-start
  57.4 26.2 %copy-start.10 = (s32[128,6]{0,1:T(8,128)S(1)}, s32[128,6]{0,1:T(8,128)}, u32[]{:S(2)}) copy-start(s32[128,6]{0,1:T(8,128)} %param.21) | copy-start | bytes 9220
  57.4 29.1 %copy-start.12 = (bf16[2048]{0:T(1024)(128)(2,1)S(1)}, bf16[2048]{0:T(1024)(128)(2,1)}, u32[]{:S(2)}) copy-start(bf16[2048]{0:T(1024)(128)(2,1)} %param.30) | copy-start | bytes 12292
  57.4 24.6 %collective-permute-start.1 = (f32[128,2048]{1,0:T(8,128)S(1)}, f32[128,2048]{1,0:T(8,128)S(1)}, u32[]{:S(2)}, u32[]{:S(2)}) collective-permute-start(f32[128,2048]{1,0:T(8,128)S(1)} %add.92), channel_id=1, source_target_pairs={{0,2},{1,3},{2,0},{3,1},{4,6},{5,7},{6,4},{7,5},{8,10},{9,11},{10,... | collective-permute-start | bytes 3145736 | tf_op jit(solution)/shard_map/ppermute | solution.py:15
  82.2 5.5 %copy-start.3 = (f32[128,2048]{1,0:T(8,128)}, f32[128,2048]{1,0:T(8,128)S(1)}, u32[]{:S(2)}) copy-start(f32[128,2048]{1,0:T(8,128)S(1)} %add.93) | copy-start | bytes 3145732
  82.2 25.6 %collective-permute-start.2 = (f32[128,2048]{1,0:T(8,128)S(1)}, f32[128,2048]{1,0:T(8,128)}, u32[]{:S(2)}, u32[]{:S(2)}) collective-permute-start(f32[128,2048]{1,0:T(8,128)S(1)} %add.93), channel_id=1, source_target_pairs={{0,4},{1,5},{2,6},{3,7},{4,0},{5,1},{6,2},{7,3},{8,12},{9,13},{10,... | collective-permute-start | bytes 3145736 | tf_op jit(solution)/shard_map/ppermute | solution.py:15
  112.0 194.7 %copy-start.15 = (bf16[2,2048,176]{1,2,0:T(8,128)(2,1)S(1)}, bf16[2,2048,176]{1,2,0:T(8,128)(2,1)}, u32[]{:S(2)}) copy-start(bf16[2,2048,176]{1,2,0:T(8,128)(2,1)} %param.32) | copy-start | bytes 4325380
  303.5 3.2 copy-start.2
  423.8 9.9 %copy-start.16 = (bf16[2048,176]{0,1:T(8,128)(2,1)S(1)}, bf16[2048,176]{0,1:T(8,128)(2,1)}, u32[]{:S(2)}) copy-start(bf16[2048,176]{0,1:T(8,128)(2,1)} %param.35) | copy-start | bytes 2162692
  423.8 10.3 %copy-start.6 = (bf16[176,2048]{1,0:T(8,128)(2,1)S(1)}, bf16[176,2048]{1,0:T(8,128)(2,1)}, u32[]{:S(2)}) copy-start(bf16[176,2048]{1,0:T(8,128)(2,1)} %param.37) | copy-start | bytes 2162692
  423.8 10.3 %copy-start.7 = (bf16[2048,176]{0,1:T(8,128)(2,1)S(1)}, bf16[2048,176]{0,1:T(8,128)(2,1)}, u32[]{:S(2)}) copy-start(bf16[2048,176]{0,1:T(8,128)(2,1)} %param.36) | copy-start | bytes 2162692
  423.8 59.1 %all-to-all-start.1 = ((f32[32,2,32,256]{3,2,1,0:T(8,128)}), f32[32,2,32,256]{3,2,1,0:T(8,128)}, u32[]{:S(2)}, u32[]{:S(2)}) async-start(f32[32,2,32,256]{3,2,1,0:T(8,128)} %copy.124), calls=%async_computation.2 | async-start | bytes 4194304 | tf_op jit(solution)/shard_map/all_to_all | solution.py:170
  433.6 53.1 %reduce-scatter.5.cloned.1.call-start = ((), (), s32[]{:S(2)}) async-start(), calls=%async_computation.5 | async-start | bytes 1179648 | tf_op jit(solution)/shard_map/reduce_scatter | solution.py:174
  434.1 2.3 copy-start.18
  442.2 46.0 %copy-start.1 = (bf16[2048,384]{1,0:T(8,128)(2,1)S(1)}, bf16[2048,384]{1,0:T(8,128)(2,1)}, u32[]{:S(2)}) copy-start(bf16[2048,384]{1,0:T(8,128)(2,1)} %param.24) | copy-start | bytes 4718596
Sparse Core Ops, SparseCore 0:
  325.9 94.6 reduce-scatter.2
  436.9 33.1 reduce-scatter.4
